TPU v7x, 512 devices: a whole 4x4x16 slice. The times are simulated.
512 devices in a mesh: chan: 32 (over z, x_hi), seg: 16 (over y, x_lo, core).
Axes of the slice: x: 4 (x_hi: 2, x_lo: 2; x = x_hi * 2 + x_lo), y: 4, z: 16, core: 2. Of those that a mesh axis runs over, the one named last changes fastest.
Arguments:
- traces: bfloat16 [512, 16, 384], P('chan', 'seg')
- taper_len: int32 [512], P('chan'), may hold values from 1 to 192
- gather_id: int32 [512, 512], P('chan'), may hold values from 0 to 511, as said below
- offset_bin: int32 [512, 512], P('chan'), may hold values from 0 to 1, as said below
Outputs:
- stack: float32 [512, 2, 256], P(('chan', 'seg'))
Inputs may be any that keep to these rules, and one draw needn't show every extreme that they name: Channels lie on a fiber at integer positions p_0 < p_1 < ... with steps of 2 to 5; gather_id[i, j] = floor((p_i + p_j - 2 p_0) * 512 / (2 (p_last - p_0) + 1)). offset_bin[i, j] = floor(|p_i - p_j| * 2 / (p_last - p_0 + 1)) with the same positions.
All inputs are finite; a program needn't handle non-finite values.
Results may differ from a plain program's by a relative error of at most 0.0039.
Values may be sent and summed in bfloat16 or wider, within the bound.
No kernel may reach another device: no remote copies, remote signals or barrier semaphores. Data moves between devices by JAX's collectives and lax.ppermute only.
A program may use at most 64 MiB of HBM per device.

v0:
```python
import math
import jax
import jax.numpy as jnp
from jax import lax
from jax.sharding import PartitionSpec as P

LAGS = 256
OFFBINS = 2


def normalize(traces, taper_len):
    values = traces.astype(jnp.float32)
    sample_count = values.shape[2]
    power = jnp.mean(values * values, axis=2, keepdims=True)
    times = jnp.arange(sample_count).astype(jnp.float32)
    length = taper_len.astype(jnp.float32)[:, None, None]
    window = jnp.minimum(1.0, jnp.minimum((times + 1.0) / length, (sample_count - times) / length))
    return (window * values * lax.rsqrt(power + 1e-06)).astype(jnp.bfloat16)


def hankel(normed, lag_count):
    chan_count, seg_count, sample_count = normed.shape
    turned = jnp.transpose(normed, (1, 2, 0))
    padded = jnp.pad(turned, ((0, 0), (lag_count // 2, lag_count // 2), (0, 0)))
    slices = [padded[:, lag_count - k : lag_count - k + sample_count, :] for k in range(lag_count)]
    picked = jnp.stack(slices, axis=3)
    return picked.reshape(seg_count * sample_count, chan_count * lag_count)


def shards(traces, taper_len, gather_id, offset_bin):
    chan_count = traces.shape[0]
    chan_devices = lax.axis_size("chan")
    seg_devices = lax.axis_size("seg")
    bucket_count = chan_devices * seg_devices * OFFBINS
    normed = normalize(traces, taper_len)
    kernel = hankel(normed, LAGS)
    first_row = lax.axis_index("chan") * chan_count
    own_rows = first_row + jnp.arange(chan_count, dtype=jnp.int32)[None, :]
    empty = jnp.zeros((bucket_count, LAGS), jnp.float32)
    flat = lax.optimization_barrier(normed.reshape(chan_count, -1))
    piece = lax.all_gather(flat, "chan", axis=0, tiled=True)
    row_count = piece.shape[0]
    product = jnp.dot(piece, kernel, preferred_element_type=jnp.float32)
    product = product.reshape(row_count * chan_count, LAGS)
    labels = jnp.transpose(gather_id * OFFBINS + offset_bin)
    partner = jnp.arange(row_count, dtype=jnp.int32)[:, None]
    labels = jnp.where(partner == own_rows, bucket_count, labels).reshape(-1)
    total = empty.at[labels].add(product, mode="drop")
    scale = 1.0 / math.sqrt(traces.shape[2] * traces.shape[1] * seg_devices)
    stacked = (total * scale).reshape(chan_devices, seg_devices, OFFBINS, LAGS)
    stacked = jnp.transpose(stacked, (1, 0, 2, 3))
    part = lax.psum_scatter(stacked, "seg", scatter_dimension=0, tiled=True)
    part = part.reshape(chan_devices, OFFBINS, LAGS)
    result = lax.psum_scatter(part, "chan", scatter_dimension=0, tiled=True)
    return result


def solution(mesh):
    placed = (P("chan", "seg", None), P("chan"), P("chan", None), P("chan", None))
    return jax.shard_map(
        shards,
        mesh=mesh,
        in_specs=placed,
        out_specs=P(("chan", "seg"), None, None),
        check_vma=False,
    )
```

profile of v0, /device:TPU:8, one launch (start us, length us, event | category | flops | bytes accessed | tf_op | source)
XLA Modules:
  0.0 545.1 jit_solution(4039340912734101357)
XLA Ops:
  6.5 0.9 fusion.5
  7.4 0.7 convert_element_type.24
  8.1 0.8 fusion.264
  8.9 0.8 fusion.265
  10.4 0.1 constant_dynamic-update-slice_fusion.246
  10.4 0.1 constant_dynamic-update-slice_fusion.245
  10.5 0.1 constant_dynamic-update-slice_fusion.244
  10.6 0.1 constant_dynamic-update-slice_fusion.243
  10.7 0.1 constant_dynamic-update-slice_fusion.242
  10.8 0.1 constant_dynamic-update-slice_fusion.241
  10.8 0.1 constant_dynamic-update-slice_fusion.240
  10.9 0.1 constant_dynamic-update-slice_fusion.239
  11.0 0.1 constant_dynamic-update-slice_fusion.238
  11.1 0.1 constant_dynamic-update-slice_fusion.237
  11.2 0.1 constant_dynamic-update-slice_fusion.236
  11.3 0.1 constant_dynamic-update-slice_fusion.235
  11.9 0.1 constant_dynamic-update-slice_fusion.227
  12.0 0.1 constant_dynamic-update-slice_fusion.226
  12.1 0.1 constant_dynamic-update-slice_fusion.225
  12.1 0.1 constant_dynamic-update-slice_fusion.224
  12.2 0.1 constant_dynamic-update-slice_fusion.223
  12.3 0.1 constant_dynamic-update-slice_fusion.222
  12.4 0.1 constant_dynamic-update-slice_fusion.221
  12.5 0.1 constant_dynamic-update-slice_fusion.220
  12.6 0.1 constant_dynamic-update-slice_fusion.219
  12.6 0.1 constant_dynamic-update-slice_fusion.218
  12.7 0.1 constant_dynamic-update-slice_fusion.217
  12.8 0.1 constant_dynamic-update-slice_fusion.216
  13.5 0.1 constant_dynamic-update-slice_fusion.208
  13.5 0.1 constant_dynamic-update-slice_fusion.207
  13.6 0.1 constant_dynamic-update-slice_fusion.206
  13.7 0.1 constant_dynamic-update-slice_fusion.205
  20.1 0.1 constant_dynamic-update-slice_fusion.127
  30.5 0.8 copy.264
  31.3 84.6 %all_gather.3 = bf16[512,384]{1,0:T(8,128)(2,1)S(1)} all-gather(bf16[16,384]{1,0:T(8,128)(2,1)S(1)} %fusion.265), channel_id=1, replica_groups=mesh['chan'=32,'seg'=16] {'chan'}, dimensions={0}, use_global_device_ids=true | all-gather | bytes 405504 | tf_op jit(solution)/shard_map/all_gather | solution.py:41
  115.9 5.6 %fusion.261 = f32[512,4096]{1,0:T(8,128)} fusion(bf16[512,384]{1,0:T(8,128)(2,1)S(1)} %all_gather.3, bf16[384,4096]{0,1:T(8,128)(2,1)S(1)} %bitcast.1036), kind=kOutput, calls=%fused_computation.785 | convolution fusion | flops 1610612736 | bytes 11927552 | tf_op jit(solution)/shard_map/dot_general | solution.py:43
  121.5 9.3 %reshape.176 = f32[8192,256]{1,0:T(8,128)} reshape(f32[512,4096]{1,0:T(8,128)} %fusion.261) | data formatting | bytes 16777216 | tf_op jit(solution)/shard_map/reshape | solution.py:44
  130.9 0.1 copy.263
  131.0 0.2 reshape.166
  131.2 44.9 %scatter_custom_fusion = f32[1024,256]{1,0:T(8,128)S(1)} fusion(s32[8192]{0:T(1024)S(1)} %bitcast.1039, f32[8192,256]{1,0:T(8,128)} %reshape.176, f32[]{:T(128)} %constant.13.clone.1), kind=kCustom, calls=%fused_computation.258 | custom fusion | flops 2097152 | bytes 1049088 | tf_op jit(solution)/shard_map/scatter-add | solution.py:48
  176.1 0.1 broadcast_multiply_fusion
  176.2 0.6 reshape.170
  176.8 1.6 copy.265
  178.5 56.0 %reduce-scatter.2.cloned.1.call-done = f32[1,32,2,256]{3,1,2,0:T(8,128)} async-done(((f32[16,32,2,256]{3,1,2,0:T(8,128)}), f32[1,32,2,256]{3,1,2,0:T(8,128)}) %reduce-scatter.2.cloned.1.call-update) | async-done | bytes 65552 | tf_op jit(solution)/shard_map/reduce_scatter | solution.py:52
  234.5 1.5 copy.266
  236.0 1.3 dynamic-slice
  237.3 299.2 %all-reduce.4.cloned.1.call-done = f32[32,2,256]{2,1,0:T(2,128)} async-done(((f32[32,2,256]{2,1,0:T(2,128)}), f32[32,2,256]{2,1,0:T(2,128)}) %all-reduce.4.cloned.1.call-update) | async-done | bytes 65552
  536.5 1.8 constant_dynamic-slice_fusion
  (242 shorter events, 18.5 us)
Async XLA Ops:
  6.5 13.5 %copy-start = (bf16[16,1,384]{2,0,1:T(8,128)(2,1)S(1)}, bf16[16,1,384]{2,0,1:T(8,128)(2,1)}, u32[]{:S(2)}) copy-start(bf16[16,1,384]{2,0,1:T(8,128)(2,1)} %param.4) | copy-start | bytes 36868
  6.5 227.9 %reduce-scatter.2.cloned.1.call-start = ((), (), s32[]{:S(2)}) async-start(), calls=%async_computation.1 | async-start | bytes 1114112 | tf_op jit(solution)/shard_map/reduce_scatter | solution.py:52
  121.5 9.3 %copy-start.1 = (s32[16,512]{1,0:T(8,128)S(1)}, s32[16,512]{1,0:T(8,128)}, u32[]{:S(2)}) copy-start(s32[16,512]{1,0:T(8,128)} %param.7) | copy-start | bytes 98308
  121.5 9.3 %copy-start.2 = (s32[16,512]{1,0:T(8,128)S(1)}, s32[16,512]{1,0:T(8,128)}, u32[]{:S(2)}) copy-start(s32[16,512]{1,0:T(8,128)} %param.6) | copy-start | bytes 98308
  178.4 358.1 %all-reduce.4.cloned.1.call-start = ((), (), s32[]{:S(2)}) async-start(), calls=%async_computation.2 | async-start | bytes 131072
Sparse Core Ops, SparseCore 0:
  178.6 55.8 reduce-scatter.1
  237.6 298.8 all-reduce.3
where the time goes:
time: 546 us; the launch traced here: 545 us
  waiting for transfers between devices  355 us (65%)
  blocking collectives  84.6 us (15%)
  other arithmetic  48.3 us (9%)
  local copies, waits for them, and re-layouts  37.7 us (7%)
  between operations  13.6 us (2%)
  matrix products  5.6 us (1%)
    unnamed x3, waiting for transfers between devices  299 us
    all_gather x1, blocking collectives, shards(): piece = lax.all_gather(flat, 'chan', axis=0, tiled=True)  84.6 us
    reduce_scatter x1, waiting for transfers between devices, shards(): part = lax.psum_scatter(stacked, 'seg', scatter_dimension=0, tiled=True)  56 us
    scatter-add x1, other arithmetic, shards(): total = empty.at[labels].add(product, mode='drop')  44.9 us
    unnamed x262, local copies, waits for them, and re-layouts  23.6 us
  transfers between devices with their start and end apart: 2, of which 2 were waited for; matrix products, arithmetic and copies ran while one was open for 0% of the time, Pallas kernels for 0%

commit v1 on v0

--- a/solution.py
+++ b/solution.py
@@ -38,7 +38,13 @@
     own_rows = first_row + jnp.arange(chan_count, dtype=jnp.int32)[None, :]
     empty = jnp.zeros((bucket_count, LAGS), jnp.float32)
     flat = lax.optimization_barrier(normed.reshape(chan_count, -1))
-    piece = lax.all_gather(flat, "chan", axis=0, tiled=True)
+    pool = []
+    for _ in range(lax.psum(1, "chan")):
+        pool.append(flat)
+    piece = jnp.concatenate(
+        lax.all_to_all(jnp.stack(pool, axis=0), axis_name="chan", split_axis=0, concat_axis=0),
+        axis=0,
+    )
     row_count = piece.shape[0]
     product = jnp.dot(piece, kernel, preferred_element_type=jnp.float32)
     product = product.reshape(row_count * chan_count, LAGS)

time: 546 us -> 493 us (0.903)
  blocking collectives: 84.6 us -> 0 us
  starting transfers between devices: 0.04 us -> 18 us
  waiting for transfers between devices: 355 us -> 363 us
    all_gather x1 -> x0, blocking collectives: 84.6 us -> none  [shards(): piece = lax.all_gather(flat, 'chan', axis=0, tiled=True)]
    all_to_all x0 -> x1, starting transfers between devices: none -> 17.9 us  [shards(): lax.all_to_all(jnp.stack(pool, axis=0), axis_name='chan', split_axis=0, c...]
    reduce_scatter x1, waiting for transfers between devices: 56 us -> 63.5 us  [shards(): part = lax.psum_scatter(stacked, 'seg', scatter_dimension=0, tiled=True)]
    unnamed x262 -> x258, local copies, waits for them, and re-layouts: 23.6 us -> 23.6 us
  transfers between devices with their start and end apart: 2 -> 3, of which waited for: 2 -> 2; matrix products, arithmetic and copies ran while one was open for 0% -> 6% of each run, Pallas kernels for 0% -> 0%
where the time goes in v1:
time: 493 us; the launch traced here: 492 us
  waiting for transfers between devices  363 us (74%)
  other arithmetic  51 us (10%)
  local copies, waits for them, and re-layouts  41.5 us (8%)
  starting transfers between devices  18 us (4%)
  between operations  13.6 us (3%)
  matrix products  5.58 us (1%)
    unnamed x3, waiting for transfers between devices  299 us
    reduce_scatter x1, waiting for transfers between devices, shards(): part = lax.psum_scatter(stacked, 'seg', scatter_dimension=0, tiled=True)  63.5 us
    scatter-add x1, other arithmetic, shards(): total = empty.at[labels].add(product, mode='drop')  44.9 us
    unnamed x258, local copies, waits for them, and re-layouts  23.6 us
    all_to_all x1, starting transfers between devices, shards(): lax.all_to_all(jnp.stack(pool, axis=0), axis_name='chan', split_axis=0, c...  17.9 us
  transfers between devices with their start and end apart: 3, of which 2 were waited for; matrix products, arithmetic and copies ran while one was open for 6% of the time, Pallas kernels for 0%

profile of v1, /device:TPU:8, one launch (start us, length us, event | category | flops | bytes accessed | tf_op | source)
XLA Modules:
  0.0 492.3 jit_solution(4138335215433166690)
XLA Ops:
  6.5 0.9 fusion.5
  7.4 0.7 convert_element_type.24
  8.1 0.8 fusion.265
  8.9 0.8 stack.806
  9.7 17.9 %all-to-all-start = ((bf16[32,16,384]{2,1,0:T(8,128)(2,1)}), bf16[32,16,384]{2,1,0:T(8,128)(2,1)S(1)}, u32[]{:S(2)}, u32[]{:S(2)}) async-start(bf16[32,16,384]{2,1,0:T(8,128)(2,1)} %stack.806), calls=%async_computation | async-start | bytes 786432 | tf_op jit(solution)/shard_map/all_to_all | solution.py:45
  27.7 0.8 fusion.264
  29.0 0.1 constant_dynamic-update-slice_fusion.248
  29.0 0.1 constant_dynamic-update-slice_fusion.247
  29.1 0.1 constant_dynamic-update-slice_fusion.246
  29.2 0.1 constant_dynamic-update-slice_fusion.245
  29.3 0.1 constant_dynamic-update-slice_fusion.244
  29.4 0.1 constant_dynamic-update-slice_fusion.243
  29.4 0.1 constant_dynamic-update-slice_fusion.242
  29.5 0.1 constant_dynamic-update-slice_fusion.241
  30.2 0.1 constant_dynamic-update-slice_fusion.233
  30.3 0.1 constant_dynamic-update-slice_fusion.232
  30.3 0.1 constant_dynamic-update-slice_fusion.231
  30.4 0.1 constant_dynamic-update-slice_fusion.230
  30.5 0.1 constant_dynamic-update-slice_fusion.229
  30.6 0.1 constant_dynamic-update-slice_fusion.228
  30.7 0.1 constant_dynamic-update-slice_fusion.227
  30.8 0.1 constant_dynamic-update-slice_fusion.226
  30.8 0.1 constant_dynamic-update-slice_fusion.225
  30.9 0.1 constant_dynamic-update-slice_fusion.224
  31.0 0.1 constant_dynamic-update-slice_fusion.223
  31.1 0.1 constant_dynamic-update-slice_fusion.222
  31.7 0.1 constant_dynamic-update-slice_fusion.214
  31.8 0.1 constant_dynamic-update-slice_fusion.213
  31.9 0.1 constant_dynamic-update-slice_fusion.212
  32.0 0.1 constant_dynamic-update-slice_fusion.211
  32.1 0.1 constant_dynamic-update-slice_fusion.210
  38.8 0.1 constant_dynamic-update-slice_fusion.127
  49.3 0.8 copy.264
  50.1 1.4 bitcast_select_fusion
  51.5 1.6 copy.263
  53.1 1.7 reshape.171
  54.8 1.4 compare_select_fusion
  56.2 5.6 %fusion.261 = f32[512,4096]{1,0:T(8,128)} fusion(bf16[512,384]{1,0:T(8,128)(2,1)S(1)} %bitcast.1039, bf16[384,4096]{0,1:T(8,128)(2,1)S(1)} %bitcast.1037), kind=kOutput, calls=%fused_computation.785 | convolution fusion | flops 1610612736 | bytes 11927552 | tf_op jit(solution)/shard_map/dot_general | solution.py:49
  61.8 9.3 %reshape.182 = f32[8192,256]{1,0:T(8,128)} reshape(f32[512,4096]{1,0:T(8,128)} %fusion.261) | data formatting | bytes 16777216 | tf_op jit(solution)/shard_map/reshape | solution.py:50
  71.1 44.9 %scatter_custom_fusion = f32[1024,256]{1,0:T(8,128)S(1)} fusion(s32[8192]{0:T(1024)} %bitcast.1041, f32[8192,256]{1,0:T(8,128)} %reshape.182, f32[]{:T(128)} %constant.13.clone.1), kind=kCustom, calls=%fused_computation.258 | custom fusion | flops 2097152 | bytes 1049088 | tf_op jit(solution)/shard_map/scatter-add | solution.py:54
  115.9 0.1 broadcast_multiply_fusion
  116.0 0.6 reshape.176
  116.7 1.6 copy.265
  118.3 63.5 %reduce-scatter.2.cloned.1.call-done = f32[1,32,2,256]{3,1,2,0:T(8,128)} async-done(((f32[16,32,2,256]{3,1,2,0:T(8,128)}), f32[1,32,2,256]{3,1,2,0:T(8,128)}) %reduce-scatter.2.cloned.1.call-update) | async-done | bytes 65552 | tf_op jit(solution)/shard_map/reduce_scatter | solution.py:58
  181.9 1.5 copy.266
  183.4 1.3 dynamic-slice
  184.7 299.0 %all-reduce.4.cloned.1.call-done = f32[32,2,256]{2,1,0:T(2,128)} async-done(((f32[32,2,256]{2,1,0:T(2,128)}), f32[32,2,256]{2,1,0:T(2,128)}) %all-reduce.4.cloned.1.call-update) | async-done | bytes 65552
  483.7 1.8 constant_dynamic-slice_fusion
  (240 shorter events, 18.7 us)
Async XLA Ops:
  6.5 32.3 %copy-start = (bf16[16,1,384]{2,0,1:T(8,128)(2,1)S(1)}, bf16[16,1,384]{2,0,1:T(8,128)(2,1)}, u32[]{:S(2)}) copy-start(bf16[16,1,384]{2,0,1:T(8,128)(2,1)} %param.4) | copy-start | bytes 36868
  9.7 46.5 %all-to-all-start = ((bf16[32,16,384]{2,1,0:T(8,128)(2,1)}), bf16[32,16,384]{2,1,0:T(8,128)(2,1)S(1)}, u32[]{:S(2)}, u32[]{:S(2)}) async-start(bf16[32,16,384]{2,1,0:T(8,128)(2,1)} %stack.806), calls=%async_computation | async-start | bytes 786432 | tf_op jit(solution)/shard_map/all_to_all | solution.py:45
  27.6 154.2 %reduce-scatter.2.cloned.1.call-start = ((), (), s32[]{:S(2)}) async-start(), calls=%async_computation.2 | async-start | bytes 1114112 | tf_op jit(solution)/shard_map/reduce_scatter | solution.py:58
  118.3 365.4 %all-reduce.4.cloned.1.call-start = ((), (), s32[]{:S(2)}) async-start(), calls=%async_computation.3 | async-start | bytes 131072
Sparse Core Ops, SparseCore 0:
  118.4 63.4 reduce-scatter.1
  185.0 298.6 all-reduce.3
